TPU v7x, 256 devices: a whole 4x4x8 slice. The times are simulated.
256 devices in a mesh: scen: 64 (over y, x, z_hi, core), trade: 4 (over z_lo).
Axes of the slice: x: 4, y: 4, z: 8 (z_hi: 2, z_lo: 4; z = z_hi * 4 + z_lo), core: 2. Of those that a mesh axis runs over, the one named last changes fastest.
Arguments:
- payoffs: float32 [12, 12, 12, 4, 8192], P(None, None, None, 'trade', 'scen'), may hold values from -4 to 4
- sweep_counts: int32 [4, 8192], P('trade', 'scen'), may hold values from 1 to 6
- netting_map: int32 [4, 8192], P('trade'), may hold values from 0 to 511
- type_lengths: int32 [8], replicated, may hold values from 1 to 8192, 32768 in all
- type_diffusion: float32 [8], replicated, may hold values from 0.02 to 0.15
- type_discount: float32 [8], replicated, may hold values from 0.01 to 0.12
- factors: float32 [3, 8192], P(None, 'scen'), may hold values from -1 to 1
Outputs:
- exposures: float32 [8192, 512], P('scen', 'trade')
- allocation: float32 [4, 8192], P('trade', 'scen')
All inputs are finite; a program needn't handle non-finite values.
Results may differ from a plain program's by a relative error of at most 0.0055.
Values may be sent and summed in bfloat16 or wider, within the bound.
No kernel may reach another device: no remote copies, remote signals or barrier semaphores. Data moves between devices by JAX's collectives and lax.ppermute only.
A program may use at most 128 MiB of HBM per device.

v0:
```python
import jax
import jax.numpy as jnp
from jax import lax
from jax.sharding import PartitionSpec as P

GRID = 12
NETS = 512
TYPES = 8
MAX_SWEEPS = 6


def cheb_matrix():
    intervals = GRID - 1
    order_index = jnp.arange(GRID, dtype=jnp.float32)
    end_weights = jnp.where((order_index == 0) | (order_index == intervals), 0.5, 1.0).astype(
        jnp.float32
    )
    angles = jnp.pi * order_index[:, None] * order_index[None, :] / intervals
    return 2.0 / intervals * end_weights[:, None] * end_weights[None, :] * jnp.cos(angles)


def cheb_basis(factors):
    factor_basis = []
    for column in range(3):
        point = factors[column]
        recurrence = [jnp.ones_like(point), point]
        for degree in range(2, GRID):
            recurrence.append(2.0 * point * recurrence[-1] - recurrence[-2])
        factor_basis.append(jnp.stack(recurrence[:GRID], 0))
    product = factor_basis[0][:, None, None, :] * factor_basis[1][None, :, None, :]
    product = product * factor_basis[2][None, None, :, :]
    return product.reshape(GRID * GRID * GRID, -1).astype(jnp.bfloat16)


def price(grid_values, counts, trade_index, type_lengths, type_diffusion, type_discount):
    type_ends = jnp.cumsum(type_lengths)
    type_ids = jnp.sum((trade_index[:, None] >= type_ends[None, :]).astype(jnp.int32), axis=1)
    type_hot = (type_ids[:, None] == jnp.arange(TYPES, dtype=jnp.int32)[None, :]).astype(
        jnp.float32
    )
    diffusion = jnp.sum(type_hot * type_diffusion[None, :], axis=1)
    discount = jnp.sum(type_hot * type_discount[None, :], axis=1)

    def smooth_step(degree, field):
        padded = jnp.pad(field, ((1, 1), (1, 1), (1, 1), (0, 0)))
        beside = padded[2:, 1:-1, 1:-1] + padded[:-2, 1:-1, 1:-1]
        beside = beside + padded[1:-1, 2:, 1:-1] + padded[1:-1, :-2, 1:-1]
        beside = beside + padded[1:-1, 1:-1, 2:] + padded[1:-1, 1:-1, :-2]
        updated = field + diffusion * (beside - 6.0 * field) - discount * field
        return jnp.where(degree < counts, updated, field)

    field = lax.fori_loop(0, MAX_SWEEPS, smooth_step, grid_values)
    matrix = cheb_matrix()
    field = jnp.einsum("ai,ijlp->ajlp", matrix, field, precision=lax.Precision.HIGHEST)
    field = jnp.einsum("bj,ajlp->ablp", matrix, field, precision=lax.Precision.HIGHEST)
    field = jnp.einsum("cl,ablp->abcp", matrix, field, precision=lax.Precision.HIGHEST)
    return field.reshape(GRID * GRID * GRID, -1).astype(jnp.bfloat16)


def shards(
    payoffs, sweep_counts, netting_map, type_lengths, type_diffusion, type_discount, factors
):
    trades_here = payoffs.shape[4]
    scen_index = lax.axis_index("scen")
    group_index = lax.axis_index("trade")
    block_size = trades_here * lax.axis_size("scen")
    first_trade = group_index * block_size + scen_index * trades_here
    trade_index = first_trade + jnp.arange(trades_here, dtype=jnp.int32)
    coef_local = price(
        payoffs[:, :, :, 0, :],
        sweep_counts[0],
        trade_index,
        type_lengths,
        type_diffusion,
        type_discount,
    )
    group_ids = netting_map[0]
    classes = jnp.arange(NETS, dtype=jnp.int32)
    scen_rows = factors.shape[1]
    scen_total = scen_rows * lax.axis_size("scen")
    basis_rows = cheb_basis(factors)
    values = lax.dot_general(
        basis_rows,
        lax.all_gather(coef_local, "scen", axis=1, tiled=True),
        (((0,), (0,)), ((), ())),
        preferred_element_type=jnp.float32,
    )
    set_hot = (group_ids[:, None] == classes[None, :]).astype(jnp.float32)
    partial_value = jnp.dot(values, set_hot, precision=lax.Precision.HIGHEST)
    totals = lax.psum_scatter(partial_value, "trade", scatter_dimension=1, tiled=True)
    exposures = jnp.maximum(totals, 0.0)
    every_set = lax.all_gather(exposures, "trade", axis=1, tiled=True)
    weight_rows = jnp.dot(every_set, set_hot.T, precision=lax.Precision.HIGHEST)
    alloc_terms = jnp.sum(values * weight_rows, axis=0) / scen_total
    allocation = lax.psum_scatter(alloc_terms, "scen", scatter_dimension=0, tiled=True)
    return (exposures, allocation.reshape(1, trades_here))


def solution(mesh):
    return jax.shard_map(
        shards,
        mesh=mesh,
        in_specs=(
            P(None, None, None, "trade", "scen"),
            P("trade", "scen"),
            P("trade", None),
            P(),
            P(),
            P(),
            P(None, "scen"),
        ),
        out_specs=(P("scen", "trade"), P("trade", "scen")),
        check_vma=False,
    )
```

profile of v0, /device:TPU:32, one launch (start us, length us, event | category | flops | bytes accessed | tf_op | source)
XLA Modules:
  0.0 805.9 jit_solution(13713044818506615753)
XLA Ops:
  7.3 1.3 copy.21
  8.6 0.2 reduce-window.8
  9.0 5.0 while.15
  9.0 0.1 copy.31
  9.1 0.7 fusion.45
  9.8 0.1 copy.31
  9.9 0.7 fusion.45
  10.7 0.1 copy.31
  10.8 0.7 fusion.45
  11.5 0.1 copy.31
  11.6 0.7 fusion.45
  12.3 0.1 copy.31
  12.5 0.7 fusion.45
  13.2 0.1 copy.31
  13.3 0.7 fusion.45
  14.0 1.6 fusion.19
  15.6 1.7 convolution_bitcast_fusion
  17.3 1.5 fusion.16
  18.9 0.9 convert_element_type.33
  19.8 0.2 reduce-scatter.2.cloned.1.call-start
  20.2 0.1 multiply_convert_fusion
  20.5 308.7 %all-gather.2.cloned.1.call-done = bf16[1728,8192]{1,0:T(8,128)(2,1)} async-done(((bf16[1728,128]{1,0:T(8,128)(2,1)}), bf16[1728,8192]{1,0:T(8,128)(2,1)}) %all-gather.2.cloned.1.call-update) | async-done | bytes 28311568 | tf_op jit(solution)/shard_map/all_gather | solution.py:84
  329.2 11.2 %fusion.39 = f32[128,8192]{1,0:T(8,128)S(1)} fusion(bf16[1728,128]{1,0:T(8,128)(2,1)S(1)} %convert_element_type.29, bf16[1728,8192]{1,0:T(8,128)(2,1)} %all-gather.2.cloned.1.call-done), kind=kOutput, calls=%fused_computation.97 | convolution fusion | flops 3623878656 | bytes 32948224 | tf_op jit(solution)/shard_map/dot_general | solution.py:82
  340.4 1.9 copy-done
  342.3 6.6 fusion.11
  349.0 0.6 dynamic-slice
  350.2 17.3 %reduce-scatter.2.cloned.1.call-done = f32[128,128]{1,0:T(8,128)} async-done(((f32[128,512]{1,0:T(8,128)}), f32[128,128]{1,0:T(8,128)}) %reduce-scatter.2.cloned.1.call-update) | async-done | bytes 65552 | tf_op jit(solution)/shard_map/reduce_scatter | solution.py:90
  367.5 0.8 broadcast_maximum_fusion
  368.4 14.5 %all_gather.7 = f32[128,512]{1,0:T(8,128)S(1)} all-gather(f32[128,128]{1,0:T(8,128)S(1)} %broadcast_maximum_fusion), channel_id=1, replica_groups=mesh['scen'=64,'trade'=4] {'trade'}, dimensions={1}, use_global_device_ids=true | all-gather | bytes 327680 | tf_op jit(solution)/shard_map/all_gather | solution.py:92
  382.8 11.0 %fusion.15 = f32[8192]{0:T(1024)S(1)} fusion(f32[128,8192]{1,0:T(8,128)} %copy-done, f32[128,512]{1,0:T(8,128)S(1)} %all_gather.7, s32[8192]{0:T(1024)S(1)} %bitcast.29), kind=kOutput, calls=%fused_computation.23 | convolution fusion | flops 6448734208 | bytes 4521984 | tf_op jit(solution)/shard_map/dot_general | solution.py:93
  393.9 404.6 %all-reduce.1 = f32[8192]{0:T(1024)S(1)} all-reduce(f32[8192]{0:T(1024)S(1)} %broadcast_multiply_fusion.1), channel_id=3, replica_groups=mesh['scen'=64,'trade'=4] {'scen'}, use_global_device_ids=true, to_apply=%region_8.9.clone | all-reduce | flops 8192 | bytes 65536
  798.5 0.6 dynamic-slice_bitcast_fusion
  (41 shorter events, 0.7 us)
Async XLA Ops:
  7.2 1.4 copy-start.6
  7.2 1.7 copy-start.4
  7.2 1.7 copy-start.3
  7.2 1.8 copy-start.7
  7.2 322.0 %all-gather.2.cloned.1.call-start = ((), (), s32[]{:S(2)}) async-start(), calls=%async_computation.1 | async-start | bytes 28753920 | tf_op jit(solution)/shard_map/all_gather | solution.py:84
  18.8 1.1 copy-start.2
  19.8 347.8 %reduce-scatter.2.cloned.1.call-start = ((), (), s32[]{:S(2)}) async-start(), calls=%async_computation.2 | async-start | bytes 327680 | tf_op jit(solution)/shard_map/reduce_scatter | solution.py:90
  20.5 321.8 %copy-start.5 = (s32[1,8192]{1,0:T(1,128)S(1)}, s32[1,8192]{1,0:T(1,128)}, u32[]{:S(2)}) copy-start(s32[1,8192]{1,0:T(1,128)} %param.11) | copy-start | bytes 98308
  340.4 1.9 copy-start
  342.3 6.6 copy-start.8
  368.4 25.5 %copy-start.1 = (f32[128,128]{1,0:T(8,128)}, f32[128,128]{1,0:T(8,128)S(1)}, u32[]{:S(2)}) copy-start(f32[128,128]{1,0:T(8,128)S(1)} %broadcast_maximum_fusion) | copy-start | bytes 196612
Sparse Core Ops, SparseCore 0:
  19.9 309.3 all-gather.1
  349.1 18.4 reduce-scatter.1
where the time goes:
time: 806 us
  blocking collectives  419 us (52%)
  waiting for transfers between devices  326 us (40%)
  matrix products  33.6 us (4%)
  between operations  14.9 us (2%)
    unnamed x1, blocking collectives  405 us
    all_gather x1, waiting for transfers between devices, shards(): lax.all_gather(coef_local, 'scen', axis=1, tiled=True)  309 us
    reduce_scatter x1, waiting for transfers between devices, shards(): lax.psum_scatter(partial_value, 'trade', scatter_dimension=1, tiled=True)  17.3 us
  transfers between devices with their start and end apart: 2, of which 2 were waited for; matrix products, arithmetic and copies ran while one was open for 0% of the time, Pallas kernels for 0%

commit v1 on v0

--- a/solution.py
+++ b/solution.py
@@ -81,7 +81,9 @@
     basis_rows = cheb_basis(factors)
     values = lax.dot_general(
         basis_rows,
-        lax.all_gather(coef_local, "scen", axis=1, tiled=True),
+        jnp.concatenate(
+            lax.all_to_all(jnp.stack([coef_local] * lax.axis_size("scen")), "scen", 0, 0), axis=1
+        ),
         (((0,), (0,)), ((), ())),
         preferred_element_type=jnp.float32,
     )

time: 806 us -> 1210 us (1.50)
  waiting for transfers between devices: 326 us -> 703 us
  starting transfers between devices: 0.26 us -> 14.2 us
    all_to_all x0 -> x1, waiting for transfers between devices: none -> 608 us  [shards(): lax.all_to_all(jnp.stack([coef_local] * lax.axis_size('scen')), 'scen', 0...]
    all_gather x1 -> x0, waiting for transfers between devices: 309 us -> none  [shards(): lax.all_gather(coef_local, 'scen', axis=1, tiled=True)]
    reduce_scatter x1, waiting for transfers between devices: 17.3 us -> 94.8 us  [shards(): lax.psum_scatter(partial_value, 'trade', scatter_dimension=1, tiled=True)]
    all_to_all x0 -> x1, starting transfers between devices: none -> 14 us  [shards(): lax.all_to_all(jnp.stack([coef_local] * lax.axis_size('scen')), 'scen', 0...]
where the time goes in v1:
time: 1210 us
  waiting for transfers between devices  703 us (58%)
  blocking collectives  419 us (35%)
  matrix products  33.6 us (3%)
  between operations  14.9 us (1%)
  local copies, waits for them, and re-layouts  14.8 us (1%)
  starting transfers between devices  14.2 us (1%)
    all_to_all x1, waiting for transfers between devices, shards(): lax.all_to_all(jnp.stack([coef_local] * lax.axis_size('scen')), 'scen', 0...  608 us
    unnamed x1, blocking collectives  405 us
    reduce_scatter x1, waiting for transfers between devices, shards(): lax.psum_scatter(partial_value, 'trade', scatter_dimension=1, tiled=True)  94.8 us
  transfers between devices with their start and end apart: 2, of which 2 were waited for; matrix products, arithmetic and copies ran while one was open for 0% of the time, Pallas kernels for 0%

profile of v1, /device:TPU:32, one launch (start us, length us, event | category | flops | bytes accessed | tf_op | source)
XLA Modules:
  0.0 1205.3 jit_solution(17413640995366753927)
XLA Ops:
  7.3 1.3 copy.31
  8.5 0.2 reduce-window.8
  8.7 0.1 convert_reduce_fusion
  8.8 0.1 select_reduce_fusion
  8.9 4.7 while.15
  8.9 0.1 copy.41
  9.0 0.7 fusion.47
  9.8 0.7 fusion.47
  10.6 0.7 fusion.47
  11.4 0.7 fusion.47
  12.2 0.7 fusion.47
  12.9 0.7 fusion.47
  13.6 1.6 fusion.22
  15.2 1.7 convolution_bitcast_fusion
  17.0 1.5 fusion.19
  18.5 0.1 convert_element_type.41
  18.6 9.6 stack.11
  28.2 14.0 %all-to-all-start = ((bf16[64,1728,128]{2,1,0:T(8,128)(2,1)}), bf16[64,1728,128]{2,1,0:T(8,128)(2,1)}, u32[]{:S(2)}, u32[]{:S(2)}) async-start(bf16[64,1728,128]{2,1,0:T(8,128)(2,1)} %stack.11), calls=%async_computation | async-start | bytes 56623104 | tf_op jit(solution)/shard_map/all_to_all | solution.py:85
  42.2 0.2 reduce-scatter.2.cloned.1.call-start
  42.7 0.1 multiply_convert_fusion
  42.8 0.1 convert_element_type.37
  43.0 608.1 %all-to-all-done = bf16[64,1728,128]{2,1,0:T(8,128)(2,1)} async-done(((bf16[64,1728,128]{2,1,0:T(8,128)(2,1)}), bf16[64,1728,128]{2,1,0:T(8,128)(2,1)}, u32[]{:S(2)}, u32[]{:S(2)}) %all-to-all-start) | async-done | bytes 28311584 | tf_op jit(solution)/shard_map/all_to_all | solution.py:85
  651.0 11.2 fusion.10
  662.2 1.9 copy-done.8
  664.1 6.6 fusion.14
  670.8 0.6 dynamic-slice
  672.0 94.8 %reduce-scatter.2.cloned.1.call-done = f32[128,128]{1,0:T(8,128)} async-done(((f32[128,512]{1,0:T(8,128)}), f32[128,128]{1,0:T(8,128)}) %reduce-scatter.2.cloned.1.call-update) | async-done | bytes 65552 | tf_op jit(solution)/shard_map/reduce_scatter | solution.py:92
  766.8 0.8 broadcast_maximum_fusion
  767.6 14.4 %all_gather.3 = f32[128,512]{1,0:T(8,128)S(1)} all-gather(f32[128,128]{1,0:T(8,128)S(1)} %broadcast_maximum_fusion), channel_id=1, replica_groups=mesh['scen'=64,'trade'=4] {'trade'}, dimensions={1}, use_global_device_ids=true | all-gather | bytes 327680 | tf_op jit(solution)/shard_map/all_gather | solution.py:94
  782.0 11.0 fusion.18
  793.1 404.8 %all-reduce.1 = f32[8192]{0:T(1024)S(1)} all-reduce(f32[8192]{0:T(1024)S(1)} %broadcast_multiply_fusion.1), channel_id=3, replica_groups=mesh['scen'=64,'trade'=4] {'scen'}, use_global_device_ids=true, to_apply=%region_8.9.clone | all-reduce | flops 8192 | bytes 65536
  1197.9 0.6 dynamic-slice_bitcast_fusion
  (41 shorter events, 0.7 us)
Async XLA Ops:
  7.2 1.4 copy-start.5
  7.2 1.6 copy-start.3
  7.2 1.6 copy-start.2
  7.2 1.7 copy-start.6
  28.2 14.3 %copy-start.1 = (f32[3,128]{1,0:T(4,128)S(1)}, f32[3,128]{1,0:T(4,128)}, u32[]{:S(2)}) copy-start(f32[3,128]{1,0:T(4,128)} %param.15) | copy-start | bytes 4612
  28.2 622.8 %all-to-all-start = ((bf16[64,1728,128]{2,1,0:T(8,128)(2,1)}), bf16[64,1728,128]{2,1,0:T(8,128)(2,1)}, u32[]{:S(2)}, u32[]{:S(2)}) async-start(bf16[64,1728,128]{2,1,0:T(8,128)(2,1)} %stack.11), calls=%async_computation | async-start | bytes 56623104 | tf_op jit(solution)/shard_map/all_to_all | solution.py:85
  42.2 724.6 %reduce-scatter.2.cloned.1.call-start = ((), (), s32[]{:S(2)}) async-start(), calls=%async_computation.2 | async-start | bytes 327680 | tf_op jit(solution)/shard_map/reduce_scatter | solution.py:92
  42.9 621.2 %copy-start.4 = (s32[1,8192]{1,0:T(1,128)S(1)}, s32[1,8192]{1,0:T(1,128)}, u32[]{:S(2)}) copy-start(s32[1,8192]{1,0:T(1,128)} %param.11) | copy-start | bytes 98308
  662.2 1.9 copy-start.8
  664.1 6.6 copy-start.7
  767.6 25.4 %copy-start = (f32[128,128]{1,0:T(8,128)}, f32[128,128]{1,0:T(8,128)S(1)}, u32[]{:S(2)}) copy-start(f32[128,128]{1,0:T(8,128)S(1)} %broadcast_maximum_fusion) | copy-start | bytes 196612
Sparse Core Ops, SparseCore 0:
  670.9 95.8 reduce-scatter.1
